TPU v7x, 256 devices: a whole 4x4x8 slice. The times are simulated.
256 devices in a mesh: dp: 4 (over x), expert: 64 (over z, y, core).
Axes of the slice: x: 4, y: 4, z: 8, core: 2. Of those that a mesh axis runs over, the one named last changes fastest.
Arguments:
- tokens: bfloat16 [4096, 2048], P(('dp', 'expert')), may hold values from -6 to 6
- expert_ids: int32 [4096, 8], P(('dp', 'expert')), may hold values from 0 to 127, all different within a row; in each aligned block of 16 rows (0 to 15, 16 to 31, ...) at most 2 rows name the same one
- gate_weights: float32 [4096, 8], P(('dp', 'expert')), may hold values from 0.1 to 1
- hot_experts: int32 [2], replicated, may hold values from 0 to 127, as said below
- capacity: int32 [128], replicated, may hold values from 32 to 64
- w_in: bfloat16 [128, 2048, 1536], P('expert', None, 'dp'), may hold values from -0.125 to 0.125
- w_out: bfloat16 [128, 1536, 2048], P('expert', 'dp'), may hold values from -0.15625 to 0.15625
- grad_y: bfloat16 [4096, 2048], P(('dp', 'expert')), may hold values from -1.5 to 1.5
Outputs:
- mixed: bfloat16 [4096, 2048], P(('dp', 'expert'))
- token_grad: bfloat16 [4096, 2048], P(('dp', 'expert'))
- gate_grad: float32 [4096, 8], P(('dp', 'expert'))
- grad_w_in: bfloat16 [128, 2048, 1536], P('expert', None, 'dp')
- grad_w_out: bfloat16 [128, 1536, 2048], P('expert', 'dp')
Inputs may be any that keep to these rules, and one draw needn't show every extreme that they name: `expert_ids`: among the tokens of one device no expert is named more than 2 times, a bound that some block reaches. `hot_experts`: 2 different experts; the last entry is always expert 128 - 1.
All inputs are finite; a program needn't handle non-finite values.
Results may differ from a plain program's by a relative error of at most 0.012.
Values may be sent and summed in bfloat16 or wider, within the bound.
No kernel may reach another device: no remote copies, remote signals or barrier semaphores. Data moves between devices by JAX's collectives and lax.ppermute only.
A program may use at most 128 MiB of HBM per device.

v0:
```python
import jax
import jax.numpy as jnp
from jax import lax
from jax.sharding import PartitionSpec as P


def prefix(part, axis, combine, identity):
    place = lax.axis_index(axis)
    gathered = lax.all_gather(part, axis)
    state = jnp.zeros_like(part) + jnp.asarray(identity, part.dtype)

    def one(turn, state):
        return combine(state, lax.dynamic_index_in_dim(gathered, turn, 0, False))

    return lax.fori_loop(0, place, one, state)


def silu_terms(pre_act):
    sig_val = jax.nn.sigmoid(pre_act)
    return (pre_act * sig_val, sig_val * (1.0 + pre_act * (1.0 - sig_val)))


def expert_math(rows_x, rows_g, weight_in, weight_out):
    pre_act = jnp.einsum("gerd,edh->gerh", rows_x, weight_in, preferred_element_type=jnp.float32)
    act_full, slope_val = silu_terms(pre_act)
    act_low = act_full.astype(jnp.bfloat16)
    out_part = jnp.einsum("gerh,ehd->gerd", act_low, weight_out, preferred_element_type=jnp.float32)
    back_act = jnp.einsum("gerd,ehd->gerh", rows_g, weight_out, preferred_element_type=jnp.float32)
    pre_grad = (back_act * slope_val).astype(jnp.bfloat16)
    in_part = jnp.einsum("gerh,edh->gerd", pre_grad, weight_in, preferred_element_type=jnp.float32)
    grad_in = jnp.einsum("gerd,gerh->edh", rows_x, pre_grad, preferred_element_type=jnp.float32)
    grad_out = jnp.einsum("gerh,gerd->ehd", act_low, rows_g, preferred_element_type=jnp.float32)
    stacked = jnp.stack([out_part, in_part], axis=1)
    partial_terms = lax.optimization_barrier(stacked.astype(jnp.bfloat16)).astype(jnp.float32)
    return (partial_terms, grad_in, grad_out)


def local(tokens, expert_ids, gate_weights, hot_experts, capacity, w_in, w_out, grad_y):
    highest = lax.Precision.HIGHEST
    expert_devs = lax.axis_size("expert")
    tok_rows, top_k = expert_ids.shape
    local_experts = w_in.shape[0]
    expert_total = local_experts * expert_devs
    slot_count = max(2, 3 * tok_rows * top_k // (2 * expert_total))
    feature_dim = tokens.shape[1]
    labels = jnp.arange(expert_total, dtype=jnp.int32)
    name_hit = (expert_ids[:, :, None] == labels).astype(jnp.int32)
    per_token = jnp.sum(name_hit, axis=1)
    local_counts = jnp.sum(per_token, axis=0)
    earlier = prefix(
        local_counts, "expert", lambda first, second: first + second, jnp.zeros_like(local_counts)
    )
    within_dev = jnp.cumsum(per_token, axis=0) - per_token
    rank_of = earlier[None, :] + within_dev
    is_hot = jnp.any(labels[:, None] == hot_experts[None, :], axis=1)
    keep_mask = jnp.logical_or(is_hot[None, :], rank_of < capacity[None, :]).astype(jnp.float32)
    slot_hit = (within_dev[:, :, None] == jnp.arange(slot_count, dtype=jnp.int32)).astype(
        jnp.float32
    )
    chosen = name_hit.astype(jnp.float32) * keep_mask[:, None, :]
    pick_mask = chosen[:, :, :, None] * slot_hit[:, None, :, :]
    sending = jnp.ones((expert_total,), jnp.float32)
    send_picks = pick_mask * sending[None, None, :, None]
    rows_sel = jnp.sum(send_picks, axis=1)
    gate_sel = jnp.einsum("tkes,tk->tes", send_picks, gate_weights, precision=highest)
    grad_f32 = grad_y.astype(jnp.float32)
    x_buf = jnp.einsum(
        "tes,td->esd", rows_sel.astype(jnp.bfloat16), tokens, preferred_element_type=jnp.float32
    ).astype(jnp.bfloat16)
    x_buf = x_buf.reshape(expert_devs, local_experts, slot_count, feature_dim)
    g_buf = jnp.einsum("tes,td->esd", gate_sel, grad_f32, precision=highest).astype(jnp.bfloat16)
    g_buf = g_buf.reshape(expert_devs, local_experts, slot_count, feature_dim)
    x_recv, g_recv = (
        lax.all_to_all(x_buf, "expert", split_axis=0, concat_axis=2, tiled=True),
        lax.all_to_all(g_buf, "expert", split_axis=0, concat_axis=2, tiled=True),
    )
    xg_all, gg_all = (
        lax.all_gather(x_recv, "dp", axis=0, tiled=True),
        lax.all_gather(g_recv, "dp", axis=0, tiled=True),
    )
    partial_terms, grad_wi, grad_wo = expert_math(xg_all, gg_all, w_in, w_out)
    summed = lax.psum_scatter(
        partial_terms.astype(jnp.bfloat16), "dp", scatter_dimension=0, tiled=True
    ).astype(jnp.float32)
    out_rows = summed[:, 0].astype(jnp.bfloat16)
    in_rows = summed[:, 1].astype(jnp.bfloat16)
    out_back, in_back = (
        lax.all_to_all(out_rows, "expert", split_axis=2, concat_axis=0, tiled=True),
        lax.all_to_all(in_rows, "expert", split_axis=2, concat_axis=0, tiled=True),
    )
    out_f32 = out_back.reshape(expert_total, slot_count, feature_dim).astype(jnp.float32)
    in_f32 = in_back.reshape(expert_total, slot_count, feature_dim).astype(jnp.float32)
    mixed = jnp.einsum("tes,esd->td", gate_sel, out_f32, precision=highest)
    token_grad = jnp.einsum("tes,esd->td", rows_sel, in_f32, precision=highest)
    dot_vals = jnp.einsum("td,esd->tes", grad_f32, out_f32, precision=highest)
    gate_grad = jnp.einsum("tkes,tes->tk", send_picks, dot_vals, precision=highest)
    return (
        mixed.astype(jnp.bfloat16),
        token_grad.astype(jnp.bfloat16),
        gate_grad,
        grad_wi.astype(jnp.bfloat16),
        grad_wo.astype(jnp.bfloat16),
    )


def solution(mesh):
    in_specs = (
        P(("dp", "expert"), None),
        P(("dp", "expert"), None),
        P(("dp", "expert"), None),
        P(),
        P(),
        P("expert", None, "dp"),
        P("expert", "dp", None),
        P(("dp", "expert"), None),
    )
    out_specs = (
        P(("dp", "expert"), None),
        P(("dp", "expert"), None),
        P(("dp", "expert"), None),
        P("expert", None, "dp"),
        P("expert", "dp", None),
    )
    return jax.shard_map(local, mesh=mesh, in_specs=in_specs, out_specs=out_specs, check_vma=False)
```

profile of v0, /device:TPU:1, one launch (start us, length us, event | category | flops | bytes accessed | tf_op | source)
XLA Modules:
  0.0 473.5 jit_solution(17353640763029097142)
XLA Ops:
  9.0 44.3 %all-gather.1 = s32[64,1,128]{2,1,0:T(1,128)S(1)} all-gather(s32[1,1,128]{2,1,0:T(1,128)S(1)} %bitcast.146), channel_id=2, replica_groups=mesh['dp'=4,'expert'=64] {'expert'}, dimensions={0}, use_global_device_ids=true | all-gather | bytes 33280 | tf_op jit(solution)/shard_map/all_gather | solution.py:9
  56.4 2.5 reshape.109
  59.0 2.4 copy.33
  61.4 35.9 %all_to_all.66 = bf16[64,2,2,2048]{3,1,2,0:T(2,128)(2,1)S(1)} all-to-all(bf16[64,2,2,2048]{3,1,2,0:T(2,128)(2,1)S(1)} %copy.33), channel_id=1, replica_groups=mesh['dp'=4,'expert'=64] {'expert'}, dimensions={0} | all-to-all | bytes 2097152 | tf_op jit(solution)/shard_map/all_to_all | solution.py:74
  101.1 2.5 reshape.110
  103.6 2.4 copy.35
  106.0 34.2 %all_to_all.67 = bf16[64,2,2,2048]{3,1,2,0:T(2,128)(2,1)S(1)} all-to-all(bf16[64,2,2,2048]{3,1,2,0:T(2,128)(2,1)S(1)} %copy.35), channel_id=1, replica_groups=mesh['dp'=4,'expert'=64] {'expert'}, dimensions={0} | all-to-all | bytes 2097152 | tf_op jit(solution)/shard_map/all_to_all | solution.py:75
  141.8 4.5 all-gather.5.cloned.1.call-done
  146.3 5.5 %fusion.1 = f32[2,4,128,384]{3,2,1,0:T(8,128)S(1)} fusion(bf16[4,2,128,2048]{3,2,0,1:T(8,128)(2,1)} %all-gather.5.cloned.1.call-done, bf16[2,2048,384]{2,1,0:T(8,128)(2,1)} %param.15), kind=kOutput, calls=%fused_computation.7 | convolution fusion | flops 1610612736 | bytes 8912896 | tf_op jit(solution)/shard_map/gerd,edh->gerh/dot_general | solution.py:24
  153.0 4.3 convert_bitcast_fusion.1
  157.3 42.5 %all-gather.7.cloned.1.call-done = bf16[4,2,128,2048]{3,2,0,1:T(8,128)(2,1)} async-done(((bf16[1,2,128,2048]{3,2,0,1:T(8,128)(2,1)}), bf16[4,2,128,2048]{3,2,0,1:T(8,128)(2,1)}) %all-gather.7.cloned.1.call-update) | async-done | bytes 4194320 | tf_op jit(solution)/shard_map/all_gather | solution.py:79
  199.8 5.2 %fusion.8 = bf16[4,2,128,384]{3,2,0,1:T(8,128)(2,1)S(1)} fusion(f32[2,4,128,384]{3,2,1,0:T(8,128)} %copy-done.9, bf16[4,2,128,2048]{3,2,0,1:T(8,128)(2,1)} %all-gather.7.cloned.1.call-done, bf16[2,384,2048]{2,1,0:T(8,128)(2,1)S(1)} %copy-done), kind=kOutput, calls=%fused_computation.19 | convolution fusion | flops 1614151680 | bytes 9699328 | tf_op jit(solution)/shard_map/gerd,ehd->gerh/dot_general | solution.py:28
  206.0 2.4 convert_bitcast_fusion
  208.4 6.2 %pad_maximum_fusion = bf16[4,2,2,128,2048]{4,3,0,2,1:T(8,128)(2,1)} fusion(bf16[4,1,2,128,2048]{4,3,0,2,1:T(8,128)(2,1)S(1)} %convert_bitcast_fusion, bf16[4,1,2,128,2048]{4,3,0,2,1:T(8,128)(2,1)} %convert_bitcast_fusion.1), kind=kLoop, calls=%fused_computation.1 | loop fusion | flops 4194304 | bytes 16777216 | tf_op jit(solution)/shard_map/stack | solution.py:33
  215.9 164.5 %all-reduce.3.cloned.1.call-done = bf16[4,2,2,128,2048]{4,3,0,2,1:T(8,128)(2,1)} async-done(((bf16[4,2,2,128,2048]{4,3,0,2,1:T(8,128)(2,1)}), bf16[4,2,2,128,2048]{4,3,0,2,1:T(8,128)(2,1)}) %all-reduce.3.cloned.1.call-update) | async-done | bytes 8388624
  384.8 11.0 %all-to-all-start.2 = ((bf16[1,2,128,2048]{3,1,0,2:T(2,128)(2,1)}), bf16[1,2,128,2048]{3,1,0,2:T(2,128)(2,1)S(1)}, u32[]{:S(2)}, u32[]{:S(2)}) async-start(bf16[1,2,128,2048]{3,1,0,2:T(2,128)(2,1)} %copy.37), calls=%async_computation.2 | async-start | bytes 2097152 | tf_op jit(solution)/shard_map/all_to_all | solution.py:88
  397.9 26.1 %all-to-all-done.2 = bf16[1,2,128,2048]{3,1,0,2:T(2,128)(2,1)S(1)} async-done(((bf16[1,2,128,2048]{3,1,0,2:T(2,128)(2,1)}), bf16[1,2,128,2048]{3,1,0,2:T(2,128)(2,1)S(1)}, u32[]{:S(2)}, u32[]{:S(2)}) %all-to-all-start.2) | async-done | bytes 1048608 | tf_op jit(solution)/shard_map/all_to_all | solution.py:88
  423.9 6.5 %all-to-all-start.3 = ((bf16[1,2,128,2048]{3,1,0,2:T(2,128)(2,1)}), bf16[1,2,128,2048]{3,1,0,2:T(2,128)(2,1)}, u32[]{:S(2)}, u32[]{:S(2)}) async-start(bf16[1,2,128,2048]{3,1,0,2:T(2,128)(2,1)} %copy.39), calls=%async_computation.3 | async-start | bytes 2097152 | tf_op jit(solution)/shard_map/all_to_all | solution.py:89
  430.4 6.4 %bitcast_convert_fusion.1 = bf16[2,2048,384]{2,1,0:T(8,128)(2,1)} fusion(bf16[4,2,128,2048]{3,2,0,1:T(8,128)(2,1)} %all-gather.5.cloned.1.call-done, bf16[4,2,128,384]{3,2,0,1:T(8,128)(2,1)S(1)} %copy-done.4), kind=kOutput, calls=%fused_computation.3 | convolution fusion | flops 1612185600 | bytes 8126464 | tf_op jit(solution)/shard_map/gerd,gerh->edh/dot_general | solution.py:31
  436.8 3.6 bitcast_convert_fusion
  444.1 2.4 fusion.6
  446.5 11.9 %all-to-all-done.3 = bf16[1,2,128,2048]{3,1,0,2:T(2,128)(2,1)} async-done(((bf16[1,2,128,2048]{3,1,0,2:T(2,128)(2,1)}), bf16[1,2,128,2048]{3,1,0,2:T(2,128)(2,1)}, u32[]{:S(2)}, u32[]{:S(2)}) %all-to-all-start.3) | async-done | bytes 1048608 | tf_op jit(solution)/shard_map/all_to_all | solution.py:89
  458.5 3.0 copy.74
  463.7 2.4 fusion.7
  (56 shorter events, 26.9 us)
Async XLA Ops:
  7.2 145.8 %copy-start = (bf16[2,384,2048]{2,1,0:T(8,128)(2,1)S(1)}, bf16[2,384,2048]{2,1,0:T(8,128)(2,1)}, u32[]{:S(2)}) copy-start(bf16[2,384,2048]{2,1,0:T(8,128)(2,1)} %param.16) | copy-start | bytes 9437188
  7.2 139.1 %all-gather.5.cloned.1.call-start = ((), (), s32[]{:S(2)}) async-start(), calls=%async_computation.4 | async-start | bytes 5242880 | tf_op jit(solution)/shard_map/all_gather | solution.py:78
  61.4 37.3 %copy-start.6 = (f32[16,8]{0,1:T(8,128)S(1)}, f32[16,8]{0,1:T(8,128)}, u32[]{:S(2)}) copy-start(f32[16,8]{0,1:T(8,128)} %param.12) | copy-start | bytes 1540
  61.4 37.6 %copy-start.5 = (bf16[16,2048]{1,0:T(8,128)(2,1)S(1)}, bf16[16,2048]{1,0:T(8,128)(2,1)}, u32[]{:S(2)}) copy-start(bf16[16,2048]{1,0:T(8,128)(2,1)} %param.17) | copy-start | bytes 196612
  98.7 101.2 %all-gather.7.cloned.1.call-start = ((), (), s32[]{:S(2)}) async-start(), calls=%async_computation.5 | async-start | bytes 5242880 | tf_op jit(solution)/shard_map/all_gather | solution.py:79
  141.6 238.8 %all-reduce.3.cloned.1.call-start = ((), (), s32[]{:S(2)}) async-start(), calls=%async_computation.6 | async-start | bytes 16777216
  151.8 1.1 copy-start.9
  199.8 6.2 %copy-start.2 = (bf16[2,2048,384]{2,1,0:T(8,128)(2,1)S(1)}, bf16[2,2048,384]{2,1,0:T(8,128)(2,1)}, u32[]{:S(2)}) copy-start(bf16[2,2048,384]{2,1,0:T(8,128)(2,1)} %param.15) | copy-start | bytes 9437188
  205.1 0.9 copy-start.3
  214.6 0.7 copy-start.8
  384.8 45.6 %copy-start.4 = (bf16[4,2,128,384]{3,2,0,1:T(8,128)(2,1)S(1)}, bf16[4,2,128,384]{3,2,0,1:T(8,128)(2,1)}, u32[]{:S(2)}) copy-start(bf16[4,2,128,384]{3,2,0,1:T(8,128)(2,1)} %copy-done.3) | copy-start | bytes 2359300
  384.8 39.2 %all-to-all-start.2 = ((bf16[1,2,128,2048]{3,1,0,2:T(2,128)(2,1)}), bf16[1,2,128,2048]{3,1,0,2:T(2,128)(2,1)S(1)}, u32[]{:S(2)}, u32[]{:S(2)}) async-start(bf16[1,2,128,2048]{3,1,0,2:T(2,128)(2,1)} %copy.37), calls=%async_computation.2 | async-start | bytes 2097152 | tf_op jit(solution)/shard_map/all_to_all | solution.py:88
  423.9 34.6 %all-to-all-start.3 = ((bf16[1,2,128,2048]{3,1,0,2:T(2,128)(2,1)}), bf16[1,2,128,2048]{3,1,0,2:T(2,128)(2,1)}, u32[]{:S(2)}, u32[]{:S(2)}) async-start(bf16[1,2,128,2048]{3,1,0,2:T(2,128)(2,1)} %copy.39), calls=%async_computation.3 | async-start | bytes 2097152 | tf_op jit(solution)/shard_map/all_to_all | solution.py:89
  430.4 6.4 %copy-start.7 = (bf16[4,2,128,2048]{3,2,0,1:T(8,128)(2,1)S(1)}, bf16[4,2,128,2048]{3,2,0,1:T(8,128)(2,1)}, u32[]{:S(2)}) copy-start(bf16[4,2,128,2048]{3,2,0,1:T(8,128)(2,1)} %all-gather.7.cloned.1.call-done) | copy-start | bytes 12582916
  430.4 6.4 %copy-start.10 = (f32[2,4,128,384]{3,2,1,0:T(8,128)S(1)}, f32[2,4,128,384]{3,2,1,0:T(8,128)}, u32[]{:S(2)}) copy-start(f32[2,4,128,384]{3,2,1,0:T(8,128)} %copy-done.9) | copy-start | bytes 4718596
  442.4 24.6 %copy-start.1 = (bf16[2,384,2048]{2,1,0:T(8,128)(2,1)S(1)}, bf16[2,384,2048]{2,1,0:T(8,128)(2,1)}, u32[]{:S(2)}) copy-start(bf16[2,384,2048]{2,1,0:T(8,128)(2,1)} %param.16) | copy-start | bytes 9437188
Sparse Core Ops, SparseCore 0:
  98.8 47.4 all-gather.4
  148.7 51.0 all-gather.6
  214.7 165.5 all-reduce.2
where the time goes:
time: 474 us; the launch traced here: 473 us
  waiting for transfers between devices  250 us (53%)
  blocking collectives  114 us (24%)
  matrix products  38.7 us (8%)
  local copies, waits for them, and re-layouts  31 us (7%)
  starting transfers between devices  17.7 us (4%)
  between operations  14 us (3%)
  other arithmetic  8.05 us (2%)
    unnamed x4, waiting for transfers between devices  165 us
    all_gather x1, blocking collectives, prefix(): gathered = lax.all_gather(part, axis)  44.3 us
    all_gather x1, waiting for transfers between devices, local(): lax.all_gather(g_recv, 'dp', axis=0, tiled=True)  42.5 us
    all_to_all x1, blocking collectives, local(): lax.all_to_all(x_buf, 'expert', split_axis=0, concat_axis=2, tiled=True)  35.9 us
    all_to_all x1, blocking collectives, local(): lax.all_to_all(g_buf, 'expert', split_axis=0, concat_axis=2, tiled=True)  34.2 us
    all_to_all x1, waiting for transfers between devices, local(): lax.all_to_all(out_rows, 'expert', split_axis=2, concat_axis=0, tiled=True)  26.1 us
    all_to_all x1, waiting for transfers between devices, local(): lax.all_to_all(in_rows, 'expert', split_axis=2, concat_axis=0, tiled=True)  11.9 us
    all_to_all x1, starting transfers between devices, local(): lax.all_to_all(out_rows, 'expert', split_axis=2, concat_axis=0, tiled=True)  11 us
  transfers between devices with their start and end apart: 5, of which 5 were waited for; matrix products, arithmetic and copies ran while one was open for 8% of the time, Pallas kernels for 0%

commit v1 on v0

--- a/solution.py
+++ b/solution.py
@@ -2,6 +2,7 @@
 import jax.numpy as jnp
 from jax import lax
 from jax.sharding import PartitionSpec as P
+from jax.lax import axis_index, axis_size, ppermute
 
 
 def prefix(part, axis, combine, identity):
@@ -74,10 +75,20 @@
         lax.all_to_all(x_buf, "expert", split_axis=0, concat_axis=2, tiled=True),
         lax.all_to_all(g_buf, "expert", split_axis=0, concat_axis=2, tiled=True),
     )
-    xg_all, gg_all = (
-        lax.all_gather(x_recv, "dp", axis=0, tiled=True),
-        lax.all_gather(g_recv, "dp", axis=0, tiled=True),
-    )
+
+    def _test_cards(frame):
+        n_blocks = axis_size("dp")
+        steps_seen = list(map(lambda dev: (dev, (dev + 1) % n_blocks), range(n_blocks)))
+        gallery = list(map(lambda dev: (dev, (dev - 1) % n_blocks), range(n_blocks)))
+        clean, current_block = ([frame], [frame])
+        for _ in range(n_blocks // 2):
+            clean.append(ppermute(clean[-1], "dp", steps_seen))
+        for _ in range((n_blocks - 1) // 2):
+            current_block.append(ppermute(current_block[-1], "dp", gallery))
+        front = jnp.concatenate([*clean[::-1], *current_block[1:]], axis=0)
+        return jnp.roll(front, (axis_index("dp") - n_blocks // 2) * frame.shape[0], axis=0)
+
+    xg_all, gg_all = (lax.all_gather(x_recv, "dp", axis=0, tiled=True), _test_cards(g_recv))
     partial_terms, grad_wi, grad_wo = expert_math(xg_all, gg_all, w_in, w_out)
     summed = lax.psum_scatter(
         partial_terms.astype(jnp.bfloat16), "dp", scatter_dimension=0, tiled=True

time: 474 us -> 508 us (1.072)
  blocking collectives: 114 us -> 44.3 us
  waiting for transfers between devices: 250 us -> 311 us
  local copies, waits for them, and re-layouts: 31 us -> 55.4 us
  starting transfers between devices: 17.7 us -> 35.7 us
    all_to_all x2 -> x0, blocking collectives: 70.1 us -> none  [the longest x1 35.9 us: local(): lax.all_to_all(x_buf, 'expert', split_axis=0, concat_axis=2, tiled=True)]
    ppermute x0 -> x3, waiting for transfers between devices: none -> 67.7 us  [the longest x2 67.7 us: _test_cards(): clean.append(ppermute(clean[-1], 'dp', steps_seen))]
    all_to_all x0 -> x2, waiting for transfers between devices: none -> 45.2 us  [the longest x1 25.4 us: local(): lax.all_to_all(g_buf, 'expert', split_axis=0, concat_axis=2, tiled=True)]
    all_gather x1 -> x0, waiting for transfers between devices: 42.5 us -> none  [local(): lax.all_gather(g_recv, 'dp', axis=0, tiled=True)]
    unnamed x25 -> x30, local copies, waits for them, and re-layouts: 4.19 us -> 19.7 us
    all_to_all x0 -> x2, starting transfers between devices: none -> 14.4 us  [the longest x1 7.97 us: local(): lax.all_to_all(x_buf, 'expert', split_axis=0, concat_axis=2, tiled=True)]
    unnamed x4 -> x3, waiting for transfers between devices: 165 us -> 162 us
  transfers between devices with their start and end apart: 5 -> 9, of which waited for: 5 -> 7; matrix products, arithmetic and copies ran while one was open for 8% -> 11% of each run, Pallas kernels for 0% -> 0%
where the time goes in v1:
time: 508 us; the launch traced here: 507 us
  waiting for transfers between devices  311 us (61%)
  local copies, waits for them, and re-layouts  55.4 us (11%)
  blocking collectives  44.3 us (9%)
  matrix products  38.6 us (8%)
  starting transfers between devices  35.7 us (7%)
  between operations  14.3 us (3%)
  other arithmetic  8.05 us (2%)
    unnamed x3, waiting for transfers between devices  162 us
    ppermute x2, waiting for transfers between devices, _test_cards(): clean.append(ppermute(clean[-1], 'dp', steps_seen))  67.7 us
    all_gather x1, blocking collectives, prefix(): gathered = lax.all_gather(part, axis)  44.3 us
    all_to_all x1, waiting for transfers between devices, local(): lax.all_to_all(out_rows, 'expert', split_axis=2, concat_axis=0, tiled=True)  26.1 us
    all_to_all x1, waiting for transfers between devices, local(): lax.all_to_all(g_buf, 'expert', split_axis=0, concat_axis=2, tiled=True)  25.4 us
    all_to_all x1, waiting for transfers between devices, local(): lax.all_to_all(x_buf, 'expert', split_axis=0, concat_axis=2, tiled=True)  19.8 us
    unnamed x30, local copies, waits for them, and re-layouts  19.7 us
    all_to_all x1, starting transfers between devices, local(): lax.all_to_all(out_rows, 'expert', split_axis=2, concat_axis=0, tiled=True)  10.9 us
  transfers between devices with their start and end apart: 9, of which 7 were waited for; matrix products, arithmetic and copies ran while one was open for 11% of the time, Pallas kernels for 0%

profile of v1, /device:TPU:1, one launch (start us, length us, event | category | flops | bytes accessed | tf_op | source)
XLA Modules:
  0.0 507.1 jit_solution(16171132596820194579)
XLA Ops:
  9.1 44.3 %all-gather.1 = s32[64,1,128]{2,1,0:T(1,128)S(1)} all-gather(s32[1,1,128]{2,1,0:T(1,128)S(1)} %bitcast.142), channel_id=2, replica_groups=mesh['dp'=4,'expert'=64] {'expert'}, dimensions={0}, use_global_device_ids=true | all-gather | bytes 33280 | tf_op jit(solution)/shard_map/all_gather | solution.py:10
  59.0 3.4 copy.33
  62.4 8.0 %all-to-all-start = ((bf16[64,2,2,2048]{3,1,2,0:T(2,128)(2,1)}), bf16[64,2,2,2048]{3,1,2,0:T(2,128)(2,1)}, u32[]{:S(2)}, u32[]{:S(2)}) async-start(bf16[64,2,2,2048]{3,1,2,0:T(2,128)(2,1)} %copy.33), calls=%async_computation | async-start | bytes 2097152 | tf_op jit(solution)/shard_map/all_to_all | solution.py:75
  75.3 3.4 copy.35
  78.7 19.8 %all-to-all-done = bf16[64,2,2,2048]{3,1,2,0:T(2,128)(2,1)} async-done(((bf16[64,2,2,2048]{3,1,2,0:T(2,128)(2,1)}), bf16[64,2,2,2048]{3,1,2,0:T(2,128)(2,1)}, u32[]{:S(2)}, u32[]{:S(2)}) %all-to-all-start) | async-done | bytes 1048608 | tf_op jit(solution)/shard_map/all_to_all | solution.py:75
  98.5 6.5 %all-to-all-start.1 = ((bf16[64,2,2,2048]{3,1,2,0:T(2,128)(2,1)}), bf16[64,2,2,2048]{3,1,2,0:T(2,128)(2,1)}, u32[]{:S(2)}, u32[]{:S(2)}) async-start(bf16[64,2,2,2048]{3,1,2,0:T(2,128)(2,1)} %copy.35), calls=%async_computation.1 | async-start | bytes 2097152 | tf_op jit(solution)/shard_map/all_to_all | solution.py:76
  105.0 2.5 copy.54
  107.6 25.4 %all-to-all-done.1 = bf16[64,2,2,2048]{3,1,2,0:T(2,128)(2,1)} async-done(((bf16[64,2,2,2048]{3,1,2,0:T(2,128)(2,1)}), bf16[64,2,2,2048]{3,1,2,0:T(2,128)(2,1)}, u32[]{:S(2)}, u32[]{:S(2)}) %all-to-all-start.1) | async-done | bytes 1048608 | tf_op jit(solution)/shard_map/all_to_all | solution.py:76
  136.8 45.1 %collective-permute-done = bf16[1,2,128,2048]{3,2,0,1:T(8,128)(2,1)} collective-permute-done((bf16[1,2,128,2048]{3,2,0,1:T(8,128)(2,1)}, bf16[1,2,128,2048]{3,2,0,1:T(8,128)(2,1)}, u32[]{:S(2)}, u32[]{:S(2)}) %collective-permute-start) | collective-permute-done | bytes 1048608 | tf_op jit(solution)/shard_map/ppermute | solution.py:85
  181.9 2.7 collective-permute-start.2
  184.5 22.7 %collective-permute-done.1 = bf16[1,2,128,2048]{3,2,0,1:T(8,128)(2,1)} collective-permute-done((bf16[1,2,128,2048]{3,2,0,1:T(8,128)(2,1)}, bf16[1,2,128,2048]{3,2,0,1:T(8,128)(2,1)}, u32[]{:S(2)}, u32[]{:S(2)}) %collective-permute-start.1) | collective-permute-done | bytes 1048608 | tf_op jit(solution)/shard_map/ppermute | solution.py:85
  211.8 2.6 constant_dynamic-update-slice_fusion.5
  226.1 5.5 %fusion.4 = f32[2,4,128,384]{3,2,1,0:T(8,128)S(1)} fusion(bf16[4,2,128,2048]{3,2,0,1:T(8,128)(2,1)} %all-gather.4.cloned.1.call-done, bf16[2,2048,384]{2,1,0:T(8,128)(2,1)} %param.15), kind=kOutput, calls=%fused_computation.10 | convolution fusion | flops 1610612736 | bytes 8912896 | tf_op jit(solution)/shard_map/gerd,edh->gerh/dot_general | solution.py:25
  231.6 4.4 convert_bitcast_fusion.1
  236.0 4.8 fusion.10
  244.2 6.2 %pad_maximum_fusion = bf16[4,2,2,128,2048]{4,3,0,2,1:T(8,128)(2,1)} fusion(bf16[4,1,2,128,2048]{4,3,0,2,1:T(8,128)(2,1)S(1)} %convert_bitcast_fusion, bf16[4,1,2,128,2048]{4,3,0,2,1:T(8,128)(2,1)} %convert_bitcast_fusion.1), kind=kLoop, calls=%fused_computation.1 | loop fusion | flops 4194304 | bytes 16777216 | tf_op jit(solution)/shard_map/stack | solution.py:34
  251.6 162.2 %all-reduce.3.cloned.1.call-done = bf16[4,2,2,128,2048]{4,3,0,2,1:T(8,128)(2,1)} async-done(((bf16[4,2,2,128,2048]{4,3,0,2,1:T(8,128)(2,1)}), bf16[4,2,2,128,2048]{4,3,0,2,1:T(8,128)(2,1)}) %all-reduce.3.cloned.1.call-update) | async-done | bytes 8388624
  418.2 10.9 %all-to-all-start.2 = ((bf16[1,2,128,2048]{3,1,0,2:T(2,128)(2,1)}), bf16[1,2,128,2048]{3,1,0,2:T(2,128)(2,1)S(1)}, u32[]{:S(2)}, u32[]{:S(2)}) async-start(bf16[1,2,128,2048]{3,1,0,2:T(2,128)(2,1)} %copy.37), calls=%async_computation.2 | async-start | bytes 2097152 | tf_op jit(solution)/shard_map/all_to_all | solution.py:99
  431.2 26.1 %all-to-all-done.2 = bf16[1,2,128,2048]{3,1,0,2:T(2,128)(2,1)S(1)} async-done(((bf16[1,2,128,2048]{3,1,0,2:T(2,128)(2,1)}), bf16[1,2,128,2048]{3,1,0,2:T(2,128)(2,1)S(1)}, u32[]{:S(2)}, u32[]{:S(2)}) %all-to-all-start.2) | async-done | bytes 1048608 | tf_op jit(solution)/shard_map/all_to_all | solution.py:99
  457.3 6.5 %all-to-all-start.3 = ((bf16[1,2,128,2048]{3,1,0,2:T(2,128)(2,1)}), bf16[1,2,128,2048]{3,1,0,2:T(2,128)(2,1)}, u32[]{:S(2)}, u32[]{:S(2)}) async-start(bf16[1,2,128,2048]{3,1,0,2:T(2,128)(2,1)} %copy.39), calls=%async_computation.3 | async-start | bytes 2097152 | tf_op jit(solution)/shard_map/all_to_all | solution.py:100
  463.8 6.4 %bitcast_convert_fusion = bf16[2,384,2048]{2,1,0:T(8,128)(2,1)} fusion(bf16[8,2,128,2048]{3,2,0,1:T(8,128)(2,1)} %constant_dynamic-update-slice_fusion, s32[]{:T(128)S(6)} %select_n.18, f32[2,4,128,384]{3,2,1,0:T(8,128)} %copy-done.9), kind=kOutput, calls=%fused_computation.2 | convolution fusion | flops 1614151680 | bytes 8912900 | tf_op jit(solution)/shard_map/gerh,gerd->ehd/dot_general | solution.py:33
  470.1 4.1 bitcast_convert_fusion.1
  482.3 9.5 %all-to-all-done.3 = bf16[1,2,128,2048]{3,1,0,2:T(2,128)(2,1)} async-done(((bf16[1,2,128,2048]{3,1,0,2:T(2,128)(2,1)}), bf16[1,2,128,2048]{3,1,0,2:T(2,128)(2,1)}, u32[]{:S(2)}, u32[]{:S(2)}) %all-to-all-start.3) | async-done | bytes 1048608 | tf_op jit(solution)/shard_map/all_to_all | solution.py:100
  491.8 2.9 copy.76
  (67 shorter events, 57.2 us)
Async XLA Ops:
  7.2 224.5 %copy-start = (bf16[2,384,2048]{2,1,0:T(8,128)(2,1)S(1)}, bf16[2,384,2048]{2,1,0:T(8,128)(2,1)}, u32[]{:S(2)}) copy-start(bf16[2,384,2048]{2,1,0:T(8,128)(2,1)} %param.16) | copy-start | bytes 9437188
  7.2 63.2 %copy-start.6 = (f32[16,8]{0,1:T(8,128)S(1)}, f32[16,8]{0,1:T(8,128)}, u32[]{:S(2)}) copy-start(f32[16,8]{0,1:T(8,128)} %param.12) | copy-start | bytes 1540
  7.2 63.6 %copy-start.5 = (bf16[16,2048]{1,0:T(8,128)(2,1)S(1)}, bf16[16,2048]{1,0:T(8,128)(2,1)}, u32[]{:S(2)}) copy-start(bf16[16,2048]{1,0:T(8,128)(2,1)} %param.17) | copy-start | bytes 196612
  62.4 36.1 %all-to-all-start = ((bf16[64,2,2,2048]{3,1,2,0:T(2,128)(2,1)}), bf16[64,2,2,2048]{3,1,2,0:T(2,128)(2,1)}, u32[]{:S(2)}, u32[]{:S(2)}) async-start(bf16[64,2,2,2048]{3,1,2,0:T(2,128)(2,1)} %copy.33), calls=%async_computation | async-start | bytes 2097152 | tf_op jit(solution)/shard_map/all_to_all | solution.py:75
  98.5 34.6 %all-to-all-start.1 = ((bf16[64,2,2,2048]{3,1,2,0:T(2,128)(2,1)}), bf16[64,2,2,2048]{3,1,2,0:T(2,128)(2,1)}, u32[]{:S(2)}, u32[]{:S(2)}) async-start(bf16[64,2,2,2048]{3,1,2,0:T(2,128)(2,1)} %copy.35), calls=%async_computation.1 | async-start | bytes 2097152 | tf_op jit(solution)/shard_map/all_to_all | solution.py:76
  105.0 121.1 %all-gather.4.cloned.1.call-start = ((), (), s32[]{:S(2)}) async-start(), calls=%async_computation.4 | async-start | bytes 5242880 | tf_op jit(solution)/shard_map/all_gather | solution.py:91
  107.6 306.3 %all-reduce.3.cloned.1.call-start = ((), (), s32[]{:S(2)}) async-start(), calls=%async_computation.5 | async-start | bytes 16777216
  135.6 46.3 %collective-permute-start = (bf16[1,2,128,2048]{3,2,0,1:T(8,128)(2,1)}, bf16[1,2,128,2048]{3,2,0,1:T(8,128)(2,1)}, u32[]{:S(2)}, u32[]{:S(2)}) collective-permute-start(bf16[1,2,128,2048]{3,2,0,1:T(8,128)(2,1)} %copy.55), channel_id=1, source_target_pairs={{0,64},{64,128},{128,192},{192,0},{1,65},{65,129},{129,193},{193,1... | collective-permute-start | bytes 3145736 | tf_op jit(solution)/shard_map/ppermute | solution.py:85
  181.9 25.4 %collective-permute-start.1 = (bf16[1,2,128,2048]{3,2,0,1:T(8,128)(2,1)}, bf16[1,2,128,2048]{3,2,0,1:T(8,128)(2,1)}, u32[]{:S(2)}, u32[]{:S(2)}) collective-permute-start(bf16[1,2,128,2048]{3,2,0,1:T(8,128)(2,1)} %collective-permute-done), channel_id=1, source_target_pairs={{0,64},{64,128},{128,192},{192,0},{1,65},{65,129},{129,193},{193,1... | collective-permute-start | bytes 3145736 | tf_op jit(solution)/shard_map/ppermute | solution.py:85
  181.9 32.5 %collective-permute-start.2 = (bf16[1,2,128,2048]{3,2,0,1:T(8,128)(2,1)}, bf16[1,2,128,2048]{3,2,0,1:T(8,128)(2,1)}, u32[]{:S(2)}, u32[]{:S(2)}) collective-permute-start(bf16[1,2,128,2048]{3,2,0,1:T(8,128)(2,1)} %copy.55), channel_id=1, source_target_pairs={{0,192},{64,0},{128,64},{192,128},{1,193},{65,1},{129,65},{193,129... | collective-permute-start | bytes 3145736 | tf_op jit(solution)/shard_map/ppermute | solution.py:87
  231.6 4.4 copy-start.9
  236.0 5.8 %copy-start.2 = (bf16[2,2048,384]{2,1,0:T(8,128)(2,1)S(1)}, bf16[2,2048,384]{2,1,0:T(8,128)(2,1)}, u32[]{:S(2)}) copy-start(bf16[2,2048,384]{2,1,0:T(8,128)(2,1)} %param.15) | copy-start | bytes 9437188
  240.8 1.0 copy-start.3
  250.3 0.7 copy-start.8
  418.2 39.0 %all-to-all-start.2 = ((bf16[1,2,128,2048]{3,1,0,2:T(2,128)(2,1)}), bf16[1,2,128,2048]{3,1,0,2:T(2,128)(2,1)S(1)}, u32[]{:S(2)}, u32[]{:S(2)}) async-start(bf16[1,2,128,2048]{3,1,0,2:T(2,128)(2,1)} %copy.37), calls=%async_computation.2 | async-start | bytes 2097152 | tf_op jit(solution)/shard_map/all_to_all | solution.py:99
  457.3 34.5 %all-to-all-start.3 = ((bf16[1,2,128,2048]{3,1,0,2:T(2,128)(2,1)}), bf16[1,2,128,2048]{3,1,0,2:T(2,128)(2,1)}, u32[]{:S(2)}, u32[]{:S(2)}) async-start(bf16[1,2,128,2048]{3,1,0,2:T(2,128)(2,1)} %copy.39), calls=%async_computation.3 | async-start | bytes 2097152 | tf_op jit(solution)/shard_map/all_to_all | solution.py:100
  463.7 6.4 %copy-start.4 = (bf16[4,2,128,384]{3,2,0,1:T(8,128)(2,1)S(1)}, bf16[4,2,128,384]{3,2,0,1:T(8,128)(2,1)}, u32[]{:S(2)}) copy-start(bf16[4,2,128,384]{3,2,0,1:T(8,128)(2,1)} %copy-done.3) | copy-start | bytes 2359300
  463.7 6.4 %copy-start.7 = (bf16[4,2,128,2048]{3,2,0,1:T(8,128)(2,1)S(1)}, bf16[4,2,128,2048]{3,2,0,1:T(8,128)(2,1)}, u32[]{:S(2)}) copy-start(bf16[4,2,128,2048]{3,2,0,1:T(8,128)(2,1)} %all-gather.4.cloned.1.call-done) | copy-start | bytes 12582916
  475.9 24.4 %copy-start.1 = (bf16[2,384,2048]{2,1,0:T(8,128)(2,1)S(1)}, bf16[2,384,2048]{2,1,0:T(8,128)(2,1)}, u32[]{:S(2)}) copy-start(bf16[2,384,2048]{2,1,0:T(8,128)(2,1)} %param.16) | copy-start | bytes 9437188
Sparse Core Ops, SparseCore 0:
  108.2 70.5 all-gather.3
  250.5 163.3 all-reduce.2
